TPU v7x, 32 devices: a whole 2x2x4 slice. The times are simulated.
32 devices in a mesh: seq: 8 (over z, y), exp: 4 (over x, core).
Axes of the slice: x: 2, y: 2, z: 4, core: 2. Of those that a mesh axis runs over, the one named last changes fastest.
Arguments:
- hidden: bfloat16 [4, 1024, 2048], P('exp', 'seq'), may hold values from -6 to 6
- lengths: int32 [4, 4], P('exp'), may hold values from 1 to 512, 1024 in all within a row
- attn_gain: float32 [2048], replicated, may hold values from 0 to 10
- w_qkv: bfloat16 [2048, 3, 16, 128], P(None, None, 'seq'), may hold values from -0.125 to 0.125
- w_out: bfloat16 [16, 128, 2048], P('seq'), may hold values from -0.125 to 0.125
- moe_gain: float32 [2048], replicated, may hold values from 0.5 to 1.5
- router: bfloat16 [2048, 16], replicated, may hold values from -8 to 8
- routes: int32 [4, 1024, 6], P('exp', 'seq'), may hold values from 0 to 15, all different within a row; in each aligned block of 128 rows (0 to 127, 128 to 255, ..., all dimensions but the last counted through in order) at most 56 rows name the same one
- w_gate_up: bfloat16 [32, 2, 704, 2048], P(('seq', 'exp')), may hold values from -0.125 to 0.125
- w_down: bfloat16 [32, 704, 2048], P(('seq', 'exp')), may hold values from -0.15625 to 0.15625
- final_gain: float32 [2048], replicated, may hold values from 0.5 to 1.5
- lm_head: bfloat16 [102400, 2048], P(('seq', 'exp')), may hold values from -4 to 4
Outputs:
- layer_out: bfloat16 [4, 1024, 2048], P('exp', 'seq')
- logprobs: float32 [16, 102400], P(None, ('seq', 'exp'))
Inputs may be any that keep to these rules, and one draw needn't show every extreme that they name: `routes`: in the rows of one device no expert is named by more than 56 rows; in some devices one expert is named by exactly 56 rows. `lengths`: each row sums to 1024; its largest entry is 512.
All inputs are finite; a program needn't handle non-finite values.
Results may differ from a plain program's by a relative error of at most 0.0095.
The roundings to bfloat16 on the way count: a program that leaves them out, or rounds other values in their place, can miss the bound.
Values may be sent and summed in bfloat16 or wider, within the bound.
No kernel may reach another device: no remote copies, remote signals or barrier semaphores. Data moves between devices by JAX's collectives and lax.ppermute only.
A program may use at most 128 MiB of HBM per device.

v0:
```python
import jax
import jax.numpy as jnp
from jax import lax
from jax.sharding import PartitionSpec as P

epsilon = 1e-06


def joined(value, axis, join):
    pieces = jax.tree.map(lambda part: lax.all_gather(part, axis), value)
    head = jax.tree.map(lambda part: part[0], pieces)
    tail = jax.tree.map(lambda part: part[1:], pieces)
    subtotal, _ = lax.scan(lambda subtotal, piece: (join(subtotal, piece), None), head, tail)
    return subtotal


def rms_scale(values, gain):
    widened = values.astype(jnp.float32)
    inverse = lax.rsqrt(jnp.mean(widened * widened, axis=-1, keepdims=True) + epsilon)
    return widened * inverse * gain


def segment_layout(prompt_lengths, count):
    ends = jnp.cumsum(prompt_lengths)
    starts = ends - prompt_lengths
    places = jnp.arange(count, dtype=jnp.int32)
    member = ((places[:, None] >= starts[None, :]) & (places[:, None] < ends[None, :])).astype(
        jnp.int32
    )
    numbers = jnp.arange(prompt_lengths.shape[0], dtype=jnp.int32)
    segment = jnp.sum(member * numbers[None, :], axis=1)
    offset = places - jnp.sum(member * starts[None, :], axis=1)
    return (segment, offset)


def rotary(values, positions):
    half_size = values.shape[-1] // 2
    freqs = 10000.0 ** (-2.0 * jnp.arange(half_size, dtype=jnp.float32) / values.shape[-1])
    angles = positions.astype(jnp.float32)[:, None] * freqs[None, :]
    cosine = jnp.cos(angles)[:, None, :]
    sine = jnp.sin(angles)[:, None, :]
    first_half = values[..., :half_size]
    second_half = values[..., half_size:]
    return jnp.concatenate(
        [first_half * cosine - second_half * sine, second_half * cosine + first_half * sine],
        axis=-1,
    )


def merge_softmax(earlier, later):
    highest = jnp.maximum(earlier[0], later[0])
    return (
        highest,
        earlier[1] * jnp.exp(earlier[0] - highest) + later[1] * jnp.exp(later[0] - highest),
    )


def per_device(
    hidden,
    lengths,
    attn_gain,
    w_qkv,
    w_out,
    moe_gain,
    router,
    routes,
    w_gate_up,
    w_down,
    final_gain,
    lm_head,
):
    seq_count = lax.axis_size("seq")
    group_count = lax.axis_size("exp")
    device_count = seq_count * group_count
    token_rows = hidden[0]
    tok_rows = token_rows.shape[0]
    model_width = token_rows.shape[1]
    group_tokens = tok_rows * seq_count
    head_count = w_qkv.shape[2]
    head_size = w_qkv.shape[3]
    scale_factor = head_size ** (-0.5)
    prompt_lengths = lengths[0]
    segment, offset = segment_layout(prompt_lengths, group_tokens)
    normed = rms_scale(token_rows, attn_gain).astype(jnp.bfloat16)
    qkv_weight = w_qkv.reshape(model_width, 3 * head_count * head_size)
    qkv = jnp.dot(
        lax.all_gather(normed, "seq", axis=0, tiled=True),
        qkv_weight,
        preferred_element_type=jnp.float32,
    ).reshape(group_tokens, 3, head_count, head_size)
    query = rotary(qkv[:, 0], offset).astype(jnp.bfloat16)
    keys = rotary(qkv[:, 1], offset).astype(jnp.bfloat16)
    values = qkv[:, 2].astype(jnp.bfloat16)
    block_rows = min(512, group_tokens)
    key_places = jnp.arange(group_tokens, dtype=jnp.int32)

    def one_block(block_index):
        first_row = block_index * block_rows
        block_query = lax.dynamic_slice_in_dim(query, first_row, block_rows, 0)
        block_segment = lax.dynamic_slice_in_dim(segment, first_row, block_rows, 0)
        query_places = first_row + jnp.arange(block_rows, dtype=jnp.int32)
        scores = (
            jnp.einsum("qhd,khd->hqk", block_query, keys, preferred_element_type=jnp.float32)
            * scale_factor
        )
        allowed = (block_segment[:, None] == segment[None, :]) & (
            key_places[None, :] <= query_places[:, None]
        )
        scores = jnp.where(allowed[None], scores, -1e30)
        highest = jnp.max(scores, axis=2, keepdims=True)
        weights = jnp.exp(scores - highest)
        probs = (weights / jnp.sum(weights, axis=2, keepdims=True)).astype(jnp.bfloat16)
        return jnp.einsum("hqk,khd->qhd", probs, values, preferred_element_type=jnp.float32).astype(
            jnp.bfloat16
        )

    blocks = lax.map(one_block, jnp.arange(group_tokens // block_rows, dtype=jnp.int32))
    heads_flat = blocks.reshape(group_tokens, head_count * head_size)
    regrouped = lax.all_to_all(heads_flat, "seq", split_axis=0, concat_axis=1, tiled=True)
    full_weight = lax.all_gather(w_out, "seq", axis=0, tiled=True).reshape(-1, model_width)
    mixed = jnp.dot(regrouped, full_weight, preferred_element_type=jnp.float32)
    middle = (token_rows.astype(jnp.float32) + mixed).astype(jnp.bfloat16)
    expert_in = rms_scale(middle, moe_gain).astype(jnp.bfloat16)
    logits = jnp.dot(expert_in, router, preferred_element_type=jnp.float32)
    expert_count = router.shape[1]
    token_routes = routes[0]
    top_count = token_routes.shape[1]
    expert_ids = jnp.arange(expert_count, dtype=jnp.int32)
    chosen_mask = token_routes[:, :, None] == expert_ids[None, None, :]
    chosen = jnp.sum(jnp.where(chosen_mask, logits[:, None, :], 0.0), axis=2)
    gates = jax.nn.softmax(chosen, axis=-1)
    capacity = max(2, tok_rows * top_count * 7 // (6 * expert_count))
    flat_mask = chosen_mask.reshape(tok_rows * top_count, expert_count).astype(jnp.int32)
    earlier_count = jnp.cumsum(flat_mask, axis=0) - flat_mask
    slot_index = jnp.sum(earlier_count * flat_mask, axis=1)
    target = (token_routes.reshape(-1) * capacity + slot_index).reshape(tok_rows, top_count)
    slot_total = expert_count * capacity
    placed = target[:, :, None] == jnp.arange(slot_total, dtype=jnp.int32)[None, None, :]
    dispatch_table = jnp.any(placed, axis=1).astype(jnp.bfloat16)
    slot_weights = jnp.sum(jnp.where(placed, gates[:, :, None], 0.0), axis=1)
    packed = lax.dot_general(
        dispatch_table, expert_in, (((0,), (0,)), ((), ())), preferred_element_type=jnp.float32
    ).astype(jnp.bfloat16)
    shares = device_count // expert_count
    outgoing = jnp.broadcast_to(
        packed.reshape(expert_count, 1, capacity, model_width),
        (expert_count, shares, capacity, model_width),
    )
    outgoing = outgoing.reshape(device_count, capacity, model_width)
    gate_up = w_gate_up[0]
    down_weight = w_down[0]
    arrived = lax.all_to_all(outgoing, ("seq", "exp"), split_axis=0, concat_axis=0, tiled=True)
    arrived_shape = arrived.shape
    flat_rows = arrived.reshape(-1, model_width)
    both = jnp.einsum("rd,gfd->rgf", flat_rows, gate_up, preferred_element_type=jnp.float32)
    act = (jax.nn.silu(both[:, 0]) * both[:, 1]).astype(jnp.bfloat16)
    part = jnp.dot(act, down_weight, preferred_element_type=jnp.float32).astype(jnp.bfloat16)
    returned = lax.all_to_all(
        part.reshape(arrived_shape), ("seq", "exp"), split_axis=0, concat_axis=0, tiled=True
    )
    summed = jnp.sum(
        returned.reshape(expert_count, shares, capacity, model_width).astype(jnp.float32), axis=1
    )
    summed = summed.reshape(slot_total, model_width)
    routed = jnp.dot(
        slot_weights, summed, precision=lax.Precision.HIGHEST, preferred_element_type=jnp.float32
    )
    layer_rows = (middle.astype(jnp.float32) + routed).astype(jnp.bfloat16)
    prompt_count = prompt_lengths.shape[0]
    last_places = jnp.cumsum(prompt_lengths) - 1
    here_places = lax.axis_index("seq") * tok_rows + jnp.arange(tok_rows, dtype=jnp.int32)
    select_table = (last_places[:, None] == here_places[None, :]).astype(jnp.bfloat16)
    picked = jnp.dot(select_table, layer_rows, preferred_element_type=jnp.float32)
    board = jnp.zeros((group_count * prompt_count, model_width), jnp.float32)
    board = lax.dynamic_update_slice_in_dim(board, picked, lax.axis_index("exp") * prompt_count, 0)
    last_rows = lax.psum(board, ("seq", "exp"))
    final = rms_scale(last_rows, final_gain).astype(jnp.bfloat16)
    vocab_scores = lax.dot_general(
        final, lm_head, (((1,), (1,)), ((), ())), preferred_element_type=jnp.float32
    )
    local_peak = jnp.max(vocab_scores, axis=1)
    local_total = jnp.sum(jnp.exp(vocab_scores - local_peak[:, None]), axis=1)
    global_peak, global_total = joined((local_peak, local_total), ("seq", "exp"), merge_softmax)
    logprobs = vocab_scores - (global_peak + jnp.log(global_total))[:, None]
    return (layer_rows[None], logprobs)


def solution(mesh):
    return jax.shard_map(
        per_device,
        mesh=mesh,
        in_specs=(
            P("exp", "seq", None),
            P("exp", None),
            P(),
            P(None, None, "seq", None),
            P("seq", None, None),
            P(),
            P(),
            P("exp", "seq", None),
            P(("seq", "exp"), None, None, None),
            P(("seq", "exp"), None, None),
            P(),
            P(("seq", "exp"), None),
        ),
        out_specs=(P("exp", "seq", None), P(None, ("seq", "exp"))),
        check_vma=False,
    )
```

profile of v0, /device:TPU:0, one launch (start us, length us, event | category | flops | bytes accessed | tf_op | source)
XLA Modules:
  0.0 774.0 jit_solution(13950051054370654755)
XLA Ops:
  7.2 1.4 fusion.43
  8.6 2.0 fusion.45
  10.7 0.7 all-gather.7.cloned.1.call-update
  11.4 0.8 reduce-window.10
  12.3 8.1 %reshape.273 = bf16[2048,768]{1,0:T(8,128)(2,1)} reshape(bf16[2048,3,2,128]{3,2,1,0:T(2,128)(2,1)} %param.19) | data formatting | bytes 6291456 | tf_op jit(solution)/shard_map/reshape | solution.py:85
  20.3 4.8 copy.43
  25.3 1.0 multiply_cosine_fusion
  26.3 60.7 %all-gather.5.cloned.1.call-done = bf16[1024,2048]{1,0:T(8,128)(2,1)} async-done(((bf16[128,2048]{1,0:T(8,128)(2,1)}), bf16[1024,2048]{1,0:T(8,128)(2,1)}) %all-gather.5.cloned.1.call-update) | async-done | bytes 4194320 | tf_op jit(solution)/shard_map/all_gather | solution.py:87
  86.9 6.2 fusion.34
  93.6 1.3 pad_maximum_fusion
  95.0 1.1 copy.45
  96.0 1.3 fusion.46
  97.4 1.0 copy.46
  98.4 21.8 %while.24 = (s32[]{:T(128)}, bf16[2,512,2,128]{3,2,1,0:T(2,128)(2,1)}, s32[2]{0:T(128)S(1)}, s32[1024]{0:T(1024)S(1)}, bf16[1024,2,128]{0,2,1:T(8,128)(2,1)}, /*...) while((s32[]{:T(128)}, ...), condition=%wide.region_7.8_spmd.clone, body=%wide.region_4.7_spmd.clone.sunk | while | flops 544867840 | bytes 15751407 | solution.py:117
  100.2 4.9 fusion.96
  105.0 3.1 fusion.97
  108.5 0.8 copy-done.9
  111.1 4.9 fusion.96
  115.9 3.1 fusion.97
  119.4 0.8 copy-done.9
  120.2 2.3 all_to_all.20
  122.5 4.3 all-to-all-start
  127.8 3.2 reduce-window.11
  131.6 0.6 fusion.48
  132.2 0.9 copy.53
  133.6 11.9 %all-to-all-done = bf16[8,128,256]{2,1,0:T(8,128)(2,1)} async-done(((bf16[8,128,256]{2,1,0:T(8,128)(2,1)}), bf16[8,128,256]{2,1,0:T(8,128)(2,1)}, u32[]{:S(2)}, u32[]{:S(2)}) %all-to-all-start) | async-done | bytes 524320 | tf_op jit(solution)/shard_map/all_to_all | solution.py:119
  145.4 2.0 copy.48
  147.5 73.1 %all-gather.7.cloned.1.call-done = bf16[16,128,2048]{2,1,0:T(8,128)(2,1)} async-done(((bf16[2,128,2048]{2,1,0:T(8,128)(2,1)}), bf16[16,128,2048]{2,1,0:T(8,128)(2,1)}) %all-gather.7.cloned.1.call-update) | async-done | bytes 8388624 | tf_op jit(solution)/shard_map/all_gather | solution.py:120
  220.6 4.9 multiply_reduce_fusion
  225.5 3.0 convolution_convert_fusion.1
  228.5 3.2 broadcast_in_dim.59
  231.7 163.6 %all_to_all.29 = bf16[32,56,2048]{2,1,0:T(8,128)(2,1)S(1)} all-to-all(bf16[32,56,2048]{2,1,0:T(8,128)(2,1)S(1)} %bitcast.119), channel_id=1, replica_groups=mesh['seq'=8,'exp'=4] {'seq','exp'}, dimensions={0} | all-to-all | bytes 14680064 | tf_op jit(solution)/shard_map/all_to_all | solution.py:152
  395.3 12.7 %fusion.31 = f32[1792,2,704]{0,2,1:T(8,128)S(1)} fusion(bf16[1792,2048,1]{1,0,2:T(8,128)(2,1)S(1)} %bitcast.124, bf16[1,2,704,2048]{3,2,1,0:T(8,128)(2,1)} %param.24), kind=kOutput, calls=%fused_computation.33 | convolution fusion | flops 10334765056 | bytes 23199744 | tf_op jit(solution)/shard_map/rd,gfd->rgf/dot_general | solution.py:155
  408.1 8.2 %convolution_convert_fusion = bf16[1792,2048]{1,0:T(8,128)(2,1)} fusion(bf16[1,704,2048]{2,1,0:T(8,128)(2,1)S(1)} %copy-done, f32[1792,2,704]{0,2,1:T(8,128)S(1)} %fusion.31), kind=kOutput, calls=%fused_computation.32 | convolution fusion | flops 5178621952 | bytes 20316160 | tf_op jit(solution)/shard_map/dot_general | solution.py:157
  416.3 3.9 all-to-all-start.2
  420.6 1.5 fusion.63
  422.2 1.1 select_reduce_fusion
  423.3 160.0 %all-to-all-done.2 = bf16[32,56,2048]{2,1,0:T(8,128)(2,1)} async-done(((bf16[32,56,2048]{2,1,0:T(8,128)(2,1)}), bf16[32,56,2048]{2,1,0:T(8,128)(2,1)}, u32[]{:S(2)}, u32[]{:S(2)}) %all-to-all-start.2) | async-done | bytes 7340064 | tf_op jit(solution)/shard_map/all_to_all | solution.py:158
  583.4 5.5 convert_reduce_fusion
  588.9 4.2 fusion.42
  593.4 0.7 copy-done.10
  594.1 120.0 %all-reduce.5.cloned.1.call-done = f32[16,2048]{1,0:T(8,128)} async-done(((f32[16,2048]{1,0:T(8,128)}), f32[16,2048]{1,0:T(8,128)}) %all-reduce.5.cloned.1.call-update) | async-done | bytes 131088 | tf_op jit(solution)/shard_map/psum | solution.py:176
  714.1 1.0 multiply_reduce_fusion.1
  715.2 8.4 %fusion.70 = (f32[16]{0:T(128)S(1)}, f32[16,3200]{1,0:T(8,128)S(1)}) fusion(bf16[3200,2048]{1,0:T(8,128)(2,1)} %param.27, f32[16,2048]{1,0:T(8,128)} %all-reduce.5.cloned.1.call-done, f32[2048]{0:T(1024)S(1)} %copy-done.14, f32[16]{0:T(128)S(1)} %add_rsqrt_fusion), kind=kOutput, calls=%fused_computation.115 | convolution fusion | flops 209864688 | bytes 13451392 | tf_op jit(solution)/shard_map/dot_general | solution.py:178
  723.6 0.7 copy-done.6
  725.0 39.2 %all-reduce.2 = (f32[512]{0:T(512)S(1)}, f32[512]{0:T(512)S(1)}) all-reduce(f32[512]{0:T(512)S(1)} %dynamic-update-slice, f32[512]{0:T(512)S(1)} %dynamic-update-slice.1), channel_id=2, replica_groups=mesh['seq'=8,'exp'=4] {'seq','exp'}, use_global_device_ids=true, to_apply=%add | all-reduce | flops 1024 | bytes 8192
  764.4 1.3 while.23
  765.8 1.7 broadcast_subtract_fusion
  (123 shorter events, 8.3 us)
Async XLA Ops:
  7.2 400.9 %copy-start = (bf16[1,704,2048]{2,1,0:T(8,128)(2,1)S(1)}, bf16[1,704,2048]{2,1,0:T(8,128)(2,1)}, u32[]{:S(2)}) copy-start(bf16[1,704,2048]{2,1,0:T(8,128)(2,1)} %param.25) | copy-start | bytes 8650756
  7.2 79.7 %all-gather.5.cloned.1.call-start = ((), (), s32[]{:S(2)}) async-start(), calls=%async_computation.3 | async-start | bytes 4718592 | tf_op jit(solution)/shard_map/all_gather | solution.py:87
  10.7 209.9 %all-gather.7.cloned.1.call-start = ((), (), s32[]{:S(2)}) async-start(), calls=%async_computation.4 | async-start | bytes 9437184 | tf_op jit(solution)/shard_map/all_gather | solution.py:120
  12.3 12.9 %copy-start.15 = (s32[4,1]{0,1:T(1,128)}, s32[4,1]{0,1:T(1,128)S(1)}, u32[]{:S(2)}) copy-start(s32[4,1]{0,1:T(1,128)S(1)} %reduce-window.10) | copy-start | bytes 52
  20.3 4.8 copy-start.17
  93.1 1.9 copy-start.4
  98.4 28.4 %copy-start.13 = (s32[1,128,6]{1,0,2:T(1,128)S(1)}, s32[1,128,6]{1,0,2:T(1,128)}, u32[]{:S(2)}) copy-start(s32[1,128,6]{1,0,2:T(1,128)} %param.23) | copy-start | bytes 9220
  105.0 3.1 copy-start.8
  108.5 0.8 copy-start.9
  115.9 3.1 copy-start.8
  119.4 0.8 copy-start.9
  120.2 100.4 %copy-start.3 = (bf16[1,128,2048]{2,1,0:T(8,128)(2,1)S(1)}, bf16[1,128,2048]{2,1,0:T(8,128)(2,1)}, u32[]{:S(2)}) copy-start(bf16[1,128,2048]{2,1,0:T(8,128)(2,1)} %param.16) | copy-start | bytes 1572868
  122.5 23.0 %all-to-all-start = ((bf16[8,128,256]{2,1,0:T(8,128)(2,1)}), bf16[8,128,256]{2,1,0:T(8,128)(2,1)}, u32[]{:S(2)}, u32[]{:S(2)}) async-start(bf16[8,128,256]{2,1,0:T(8,128)(2,1)} %all_to_all.20), calls=%async_computation | async-start | bytes 1048576 | tf_op jit(solution)/shard_map/all_to_all | solution.py:119
  220.6 5.0 copy-start.12
  225.5 3.0 copy-start.1
  416.3 4.3 copy-start.16
  416.3 4.3 copy-start.11
  416.3 167.0 %all-to-all-start.2 = ((bf16[32,56,2048]{2,1,0:T(8,128)(2,1)}), bf16[32,56,2048]{2,1,0:T(8,128)(2,1)}, u32[]{:S(2)}, u32[]{:S(2)}) async-start(bf16[32,56,2048]{2,1,0:T(8,128)(2,1)} %bitcast.123), calls=%async_computation.2 | async-start | bytes 14680064 | tf_op jit(solution)/shard_map/all_to_all | solution.py:158
  420.3 293.9 %all-reduce.5.cloned.1.call-start = ((), (), s32[]{:S(2)}) async-start(), calls=%async_computation.5 | async-start | bytes 262144 | tf_op jit(solution)/shard_map/psum | solution.py:176
  583.4 5.5 copy-start.2
  583.4 5.5 copy-start.7
  588.9 126.3 %copy-start.14 = (f32[2048]{0:T(1024)S(1)}, f32[2048]{0:T(1024)}, u32[]{:S(2)}) copy-start(f32[2048]{0:T(1024)} %param.26) | copy-start | bytes 24580
  593.1 130.5 %copy-start.5 = (bf16[128,2048]{1,0:T(8,128)(2,1)}, bf16[128,2048]{1,0:T(8,128)(2,1)S(1)}, u32[]{:S(2)}) copy-start(bf16[128,2048]{1,0:T(8,128)(2,1)S(1)} %fusion.42) | copy-start | bytes 1572868
  593.4 0.7 copy-start.10
  723.6 0.7 copy-start.6
Sparse Core Ops, SparseCore 0:
  10.8 76.0 all-gather.4
  89.0 131.4 all-gather.6
  594.2 119.8 all-reduce.4
where the time goes:
time: 775 us; the launch traced here: 774 us
  waiting for transfers between devices  426 us (55%)
  blocking collectives  203 us (26%)
  matrix products  65.4 us (8%)
  local copies, waits for them, and re-layouts  31.1 us (4%)
  other arithmetic  23.9 us (3%)
  between operations  14.1 us (2%)
  starting transfers between devices  8.62 us (1%)
    all_to_all x1, blocking collectives, per_device(): lax.all_to_all(outgoing, ('seq', 'exp'), split_axis=0, concat_axis=0, til...  164 us
    all_to_all x1, waiting for transfers between devices, per_device(): lax.all_to_all(part.reshape(arrived_shape), ('seq', 'exp'), split_axis=0,...  160 us
    psum x1, waiting for transfers between devices, per_device(): last_rows = lax.psum(board, ('seq', 'exp'))  120 us
    all_gather x1, waiting for transfers between devices, per_device(): lax.all_gather(w_out, 'seq', axis=0, tiled=True).reshape(-1, model_width)  73.1 us
    all_gather x1, waiting for transfers between devices, per_device(): lax.all_gather(normed, 'seq', axis=0, tiled=True)  60.7 us
    unnamed x1, blocking collectives  39.2 us
  transfers between devices with their start and end apart: 5, of which 5 were waited for; matrix products, arithmetic and copies ran while one was open for 7% of the time, Pallas kernels for 0%

commit v1 on v0

--- a/solution.py
+++ b/solution.py
@@ -45,6 +45,11 @@
         [first_half * cosine - second_half * sine, second_half * cosine + first_half * sine],
         axis=-1,
     )
+
+
+def pair_swap(value):
+    count = lax.axis_size("exp")
+    return lax.ppermute(value, "exp", [(i, i ^ 1) for i in range(count)])
 
 
 def merge_softmax(earlier, later):
@@ -117,8 +122,17 @@
     blocks = lax.map(one_block, jnp.arange(group_tokens // block_rows, dtype=jnp.int32))
     heads_flat = blocks.reshape(group_tokens, head_count * head_size)
     regrouped = lax.all_to_all(heads_flat, "seq", split_axis=0, concat_axis=1, tiled=True)
-    full_weight = lax.all_gather(w_out, "seq", axis=0, tiled=True).reshape(-1, model_width)
-    mixed = jnp.dot(regrouped, full_weight, preferred_element_type=jnp.float32)
+    core = lax.axis_index("exp") % 2
+    half_size = head_size // 2
+    own_half = lax.dynamic_slice_in_dim(w_out, core * half_size, half_size, axis=1)
+    own_weight = lax.all_gather(own_half, "seq", axis=0, tiled=True)
+    other_weight = pair_swap(own_weight)
+    regrouped = regrouped.reshape(tok_rows, -1, head_size)
+    own_heads = lax.dynamic_slice_in_dim(regrouped, core * half_size, half_size, axis=2)
+    other_heads = lax.dynamic_slice_in_dim(regrouped, (1 - core) * half_size, half_size, axis=2)
+    mixed = jnp.einsum(
+        "thd,hdo->to", own_heads, own_weight, preferred_element_type=jnp.float32
+    ) + jnp.einsum("thd,hdo->to", other_heads, other_weight, preferred_element_type=jnp.float32)
     middle = (token_rows.astype(jnp.float32) + mixed).astype(jnp.bfloat16)
     expert_in = rms_scale(middle, moe_gain).astype(jnp.bfloat16)
     logits = jnp.dot(expert_in, router, preferred_element_type=jnp.float32)
@@ -142,26 +156,31 @@
         dispatch_table, expert_in, (((0,), (0,)), ((), ())), preferred_element_type=jnp.float32
     ).astype(jnp.bfloat16)
     shares = device_count // expert_count
-    outgoing = jnp.broadcast_to(
-        packed.reshape(expert_count, 1, capacity, model_width),
-        (expert_count, shares, capacity, model_width),
-    )
-    outgoing = outgoing.reshape(device_count, capacity, model_width)
+    assert capacity % shares == 0
+    outgoing = packed.reshape(device_count, capacity // shares, model_width)
     gate_up = w_gate_up[0]
     down_weight = w_down[0]
+    other_gate_up = pair_swap(gate_up)
+    other_down = pair_swap(down_weight)
     arrived = lax.all_to_all(outgoing, ("seq", "exp"), split_axis=0, concat_axis=0, tiled=True)
     arrived_shape = arrived.shape
     flat_rows = arrived.reshape(-1, model_width)
-    both = jnp.einsum("rd,gfd->rgf", flat_rows, gate_up, preferred_element_type=jnp.float32)
-    act = (jax.nn.silu(both[:, 0]) * both[:, 1]).astype(jnp.bfloat16)
-    part = jnp.dot(act, down_weight, preferred_element_type=jnp.float32).astype(jnp.bfloat16)
+
+    def share_part(pair, down):
+        both = jnp.einsum("rd,gfd->rgf", flat_rows, pair, preferred_element_type=jnp.float32)
+        act = (jax.nn.silu(both[:, 0]) * both[:, 1]).astype(jnp.bfloat16)
+        part = jnp.dot(act, down, preferred_element_type=jnp.float32).astype(jnp.bfloat16)
+        return part.astype(jnp.float32)
+
+    part_sum = share_part(gate_up, down_weight) + share_part(other_gate_up, other_down)
     returned = lax.all_to_all(
-        part.reshape(arrived_shape), ("seq", "exp"), split_axis=0, concat_axis=0, tiled=True
-    )
-    summed = jnp.sum(
-        returned.reshape(expert_count, shares, capacity, model_width).astype(jnp.float32), axis=1
-    )
-    summed = summed.reshape(slot_total, model_width)
+        part_sum.astype(jnp.bfloat16).reshape(arrived_shape),
+        ("seq", "exp"),
+        split_axis=0,
+        concat_axis=0,
+        tiled=True,
+    )
+    summed = returned.reshape(slot_total, model_width).astype(jnp.float32)
     routed = jnp.dot(
         slot_weights, summed, precision=lax.Precision.HIGHEST, preferred_element_type=jnp.float32
     )
@@ -171,9 +190,11 @@
     here_places = lax.axis_index("seq") * tok_rows + jnp.arange(tok_rows, dtype=jnp.int32)
     select_table = (last_places[:, None] == here_places[None, :]).astype(jnp.bfloat16)
     picked = jnp.dot(select_table, layer_rows, preferred_element_type=jnp.float32)
-    board = jnp.zeros((group_count * prompt_count, model_width), jnp.float32)
-    board = lax.dynamic_update_slice_in_dim(board, picked, lax.axis_index("exp") * prompt_count, 0)
-    last_rows = lax.psum(board, ("seq", "exp"))
+    board = jnp.zeros((group_count * prompt_count, model_width), jnp.bfloat16)
+    board = lax.dynamic_update_slice_in_dim(
+        board, picked.astype(jnp.bfloat16), lax.axis_index("exp") * prompt_count, 0
+    )
+    last_rows = lax.psum(board, ("seq", "exp")).astype(jnp.float32)
     final = rms_scale(last_rows, final_gain).astype(jnp.bfloat16)
     vocab_scores = lax.dot_general(
         final, lm_head, (((1,), (1,)), ((), ())), preferred_element_type=jnp.float32

time: 775 us -> 639 us (0.82)
  blocking collectives: 203 us -> 40.8 us
  waiting for transfers between devices: 426 us -> 441 us
  local copies, waits for them, and re-layouts: 31.1 us -> 45.9 us
  other arithmetic: 23.9 us -> 11.9 us
    all_to_all x1 -> x0, blocking collectives: 164 us -> none  [per_device(): lax.all_to_all(outgoing, ('seq', 'exp'), split_axis=0, concat_axis=0, til...]
    all_to_all x1 -> x2, waiting for transfers between devices: 160 us -> 186 us  [the longest x1 93.3 us: per_device(): lax.all_to_all(outgoing, ('seq', 'exp'), split_axis=0, concat_axis=0, til...]
    reshape x0 -> x4, local copies, waits for them, and re-layouts: none -> 23.4 us  [the longest x1 5.92 us: per_device(): flat_rows = arrived.reshape(-1, model_width)]
    all_gather x1, waiting for transfers between devices: 73.1 us -> 64.4 us  [per_device(): own_weight = lax.all_gather(own_half, 'seq', axis=0, tiled=True)]
    dot_general x3 -> x6, matrix products: 25.9 us -> 34.1 us  [the longest x2 17.8 us: share_part(): jnp.einsum('rd,gfd->rgf', flat_rows, pair, preferred_element_type=jnp.flo...]
  transfers between devices with their start and end apart: 5 -> 9, of which waited for: 5 -> 6; matrix products, arithmetic and copies ran while one was open for 7% -> 12% of each run, Pallas kernels for 0% -> 0%
where the time goes in v1:
time: 639 us; the launch traced here: 637 us
  waiting for transfers between devices  441 us (69%)
  matrix products  69.6 us (11%)
  local copies, waits for them, and re-layouts  45.9 us (7%)
  blocking collectives  40.8 us (6%)
  between operations  14.3 us (2%)
  starting transfers between devices  12.4 us (2%)
  other arithmetic  11.9 us (2%)
    psum x1, waiting for transfers between devices, per_device(): last_rows = lax.psum(board, ('seq', 'exp')).astype(jnp.float32)  117 us
    all_to_all x1, waiting for transfers between devices, per_device(): lax.all_to_all(outgoing, ('seq', 'exp'), split_axis=0, concat_axis=0, til...  93.3 us
    all_to_all x1, waiting for transfers between devices, per_device(): lax.all_to_all(part_sum.astype(jnp.bfloat16).reshape(arrived_shape), ('se...  92.8 us
    all_gather x1, waiting for transfers between devices, per_device(): own_weight = lax.all_gather(own_half, 'seq', axis=0, tiled=True)  64.4 us
    all_gather x1, waiting for transfers between devices, per_device(): lax.all_gather(normed, 'seq', axis=0, tiled=True)  61.2 us
    unnamed x1, blocking collectives  40.8 us
    dot_general x2, matrix products, share_part(): jnp.einsum('rd,gfd->rgf', flat_rows, pair, preferred_element_type=jnp.flo...  17.8 us
  transfers between devices with their start and end apart: 9, of which 6 were waited for; matrix products, arithmetic and copies ran while one was open for 12% of the time, Pallas kernels for 0%

profile of v1, /device:TPU:0, one launch (start us, length us, event | category | flops | bytes accessed | tf_op | source)
XLA Modules:
  0.0 637.5 jit_solution(17529622819611426284)
XLA Ops:
  7.2 1.3 fusion.48
  8.6 2.1 fusion.50
  10.7 0.8 constant_dynamic-slice_fusion.2
  11.8 8.0 %reshape.269 = bf16[2048,768]{1,0:T(8,128)(2,1)} reshape(bf16[2048,3,2,128]{3,2,1,0:T(2,128)(2,1)} %param.19) | data formatting | bytes 6291456 | tf_op jit(solution)/shard_map/reshape | solution.py:90
  19.8 4.8 copy.43
  24.7 1.0 multiply_cosine_fusion
  25.7 61.2 %all-gather.5.cloned.1.call-done = bf16[1024,2048]{1,0:T(8,128)(2,1)} async-done(((bf16[128,2048]{1,0:T(8,128)(2,1)}), bf16[1024,2048]{1,0:T(8,128)(2,1)}) %all-gather.5.cloned.1.call-update) | async-done | bytes 4194320 | tf_op jit(solution)/shard_map/all_gather | solution.py:92
  86.9 6.2 fusion.31
  93.6 1.2 copy-done.4
  95.2 1.4 fusion.51
  96.8 64.4 %all-gather.7.cloned.1.call-done = bf16[16,64,2048]{2,1,0:T(8,128)(2,1)} async-done(((bf16[2,64,2048]{2,1,0:T(8,128)(2,1)}), bf16[16,64,2048]{2,1,0:T(8,128)(2,1)}) %all-gather.7.cloned.1.call-update) | async-done | bytes 4194320 | tf_op jit(solution)/shard_map/all_gather | solution.py:128
  161.3 17.8 %while.24 = (s32[]{:T(128)}, bf16[2,512,2,128]{3,2,1,0:T(2,128)(2,1)S(1)}, s32[2]{0:T(128)S(1)}, s32[1024]{0:T(1024)S(1)}, bf16[1024,2,128]{0,2,1:T(8,128)(2,1)S...) while((s32[]{:T(128)}, ...), condition=%wide.region_7.8_spmd.clone, body=%wide.region_4.7_spmd.clone.sunk | while | flops 544867840 | bytes 11557047 | solution.py:122
  161.3 0.6 dynamic_slice.72
  162.6 0.6 fusion.116
  163.2 3.7 fusion.117
  166.9 2.9 fusion.118
  170.2 0.6 dynamic_slice.72
  171.5 0.6 fusion.116
  172.1 3.7 fusion.117
  175.8 2.9 fusion.118
  179.1 1.1 all_to_all.18
  180.2 3.7 all-to-all-start
  184.3 1.7 reduce-window.11
  186.7 0.5 fusion.33
  187.1 12.0 %all-to-all-done = bf16[8,128,256]{2,1,0:T(8,128)(2,1)S(1)} async-done(((bf16[8,128,256]{2,1,0:T(8,128)(2,1)}), bf16[8,128,256]{2,1,0:T(8,128)(2,1)S(1)}, u32[]{:S(2)}, u32[]{:S(2)}) %all-to-all-start) | async-done | bytes 524320 | tf_op jit(solution)/shard_map/all_to_all | solution.py:124
  199.4 2.9 convolution_bitcast_fusion.1
  202.4 3.1 multiply_reduce_fusion
  205.5 3.0 convolution_convert_fusion
  208.5 5.8 reshape.272
  214.3 3.7 all-to-all-start.1
  218.6 93.3 %all-to-all-done.1 = bf16[32,28,2048]{2,1,0:T(8,128)(2,1)} async-done(((bf16[32,28,2048]{2,1,0:T(8,128)(2,1)}), bf16[32,28,2048]{2,1,0:T(8,128)(2,1)}, u32[]{:S(2)}, u32[]{:S(2)}) %all-to-all-start.1) | async-done | bytes 3670048 | tf_op jit(solution)/shard_map/all_to_all | solution.py:165
  311.9 5.9 reshape.292
  317.8 9.4 %fusion.76 = f32[896,2,704]{0,2,1:T(8,128)S(1)} fusion(bf16[896,2048,1]{1,0,2:T(8,128)(2,1)} %reshape.292, bf16[1,2,704,2048]{3,2,1,0:T(8,128)(2,1)} %param.24), kind=kOutput, calls=%fused_computation.127 | convolution fusion | flops 5167382528 | bytes 14483456 | tf_op jit(solution)/shard_map/rd,gfd->rgf/dot_general | solution.py:170
  327.3 3.4 fusion.44
  330.7 8.4 %fusion.88 = f32[896,2,704]{0,2,1:T(8,128)S(1)} fusion(bf16[896,2048,1]{1,0,2:T(8,128)(2,1)S(1)} %copy-done.3, bf16[2,704,2048]{2,1,0:T(8,128)(2,1)} %collective-permute-done.1), kind=kOutput, calls=%fused_computation.134 | convolution fusion | flops 5167382528 | bytes 14483456 | tf_op jit(solution)/shard_map/rd,gfd->rgf/dot_general | solution.py:170
  339.2 6.9 %add_convert_fusion = bf16[896,2048]{1,0:T(8,128)(2,1)} fusion(bf16[896,2048]{1,0:T(8,128)(2,1)S(1)} %fusion.44, bf16[704,2048]{1,0:T(8,128)(2,1)} %collective-permute-done.2, f32[896,2,704]{0,2,1:T(8,128)S(1)} %fusion.88), kind=kOutput, calls=%fused_computation.31 | convolution fusion | flops 2596651008 | bytes 15269888 | tf_op jit(solution)/shard_map/dot_general | solution.py:172
  346.0 5.8 reshape.274
  351.9 4.1 all-to-all-start.2
  357.1 92.8 %all-to-all-done.2 = bf16[32,28,2048]{2,1,0:T(8,128)(2,1)} async-done(((bf16[32,28,2048]{2,1,0:T(8,128)(2,1)}), bf16[32,28,2048]{2,1,0:T(8,128)(2,1)}, u32[]{:S(2)}, u32[]{:S(2)}) %all-to-all-start.2) | async-done | bytes 3670048 | tf_op jit(solution)/shard_map/all_to_all | solution.py:176
  449.8 5.8 reshape.275
  455.7 3.9 fusion.40
  459.8 0.6 copy-done.6
  460.5 117.0 %all-reduce.5.cloned.1.call-done = bf16[16,2048]{1,0:T(8,128)(2,1)} async-done(((bf16[16,2048]{1,0:T(8,128)(2,1)}), bf16[16,2048]{1,0:T(8,128)(2,1)}) %all-reduce.5.cloned.1.call-update) | async-done | bytes 65552 | tf_op jit(solution)/shard_map/psum | solution.py:197
  577.5 1.0 fusion.54
  578.5 8.5 %fusion.87 = (f32[16]{0:T(128)S(1)}, f32[16,3200]{1,0:T(8,128)S(1)}) fusion(bf16[3200,2048]{1,0:T(8,128)(2,1)} %param.27, bf16[16,2048]{1,0:T(8,128)(2,1)} %all-reduce.5.cloned.1.call-done, f32[2048]{0:T(1024)S(1)} %copy-done.10, f32[16]{0:T(128)S(1)} %add_rsqrt_fusion), kind=kOutput, calls=%fused_computation.133 | convolution fusion | flops 209897456 | bytes 13385856 | tf_op jit(solution)/shard_map/dot_general | solution.py:199
  587.7 40.8 %all-reduce.2 = (f32[512]{0:T(512)S(1)}, f32[512]{0:T(512)S(1)}) all-reduce(f32[512]{0:T(512)S(1)} %dynamic-update-slice, f32[512]{0:T(512)S(1)} %dynamic-update-slice.1), channel_id=2, replica_groups=mesh['seq'=8,'exp'=4] {'seq','exp'}, use_global_device_ids=true, to_apply=%add | all-reduce | flops 1024 | bytes 8192
  628.8 1.3 while.23
  630.2 0.8 broadcast_subtract_fusion
  (122 shorter events, 7.4 us)
Async XLA Ops:
  7.2 3.5 copy-start
  7.2 4.4 copy-start.12
  7.2 79.7 %all-gather.5.cloned.1.call-start = ((), (), s32[]{:S(2)}) async-start(), calls=%async_computation.3 | async-start | bytes 4718592 | tf_op jit(solution)/shard_map/all_gather | solution.py:92
  10.6 150.7 %all-gather.7.cloned.1.call-start = ((), (), s32[]{:S(2)}) async-start(), calls=%async_computation.4 | async-start | bytes 4718592 | tf_op jit(solution)/shard_map/all_gather | solution.py:128
  93.1 1.7 copy-start.4
  161.3 41.1 %collective-permute-start = (bf16[16,64,2048]{2,1,0:T(8,128)(2,1)}, bf16[16,64,2048]{2,1,0:T(8,128)(2,1)}, u32[]{:S(2)}, u32[]{:S(2)}) collective-permute-start(bf16[16,64,2048]{2,1,0:T(8,128)(2,1)} %all-gather.7.cloned.1.call-done), channel_id=1, source_target_pairs={{0,1},{1,0},{2,3},{3,2},{4,5},{5,4},{6,7},{7,6},{8,9},{9,8},{10,11... | collective-permute-start | bytes 12582920 | tf_op jit(solution)/shard_map/ppermute | solution.py:52
  161.3 22.6 %copy-start.9 = (s32[1,128,6]{1,0,2:T(1,128)S(1)}, s32[1,128,6]{1,0,2:T(1,128)}, u32[]{:S(2)}) copy-start(s32[1,128,6]{1,0,2:T(1,128)} %param.23) | copy-start | bytes 9220
  180.2 18.9 %all-to-all-start = ((bf16[8,128,256]{2,1,0:T(8,128)(2,1)}), bf16[8,128,256]{2,1,0:T(8,128)(2,1)S(1)}, u32[]{:S(2)}, u32[]{:S(2)}) async-start(bf16[8,128,256]{2,1,0:T(8,128)(2,1)} %all_to_all.18), calls=%async_computation | async-start | bytes 1048576 | tf_op jit(solution)/shard_map/all_to_all | solution.py:124
  184.2 18.2 %copy-start.2 = (bf16[1,128,2048]{2,1,0:T(8,128)(2,1)S(1)}, bf16[1,128,2048]{2,1,0:T(8,128)(2,1)}, u32[]{:S(2)}) copy-start(bf16[1,128,2048]{2,1,0:T(8,128)(2,1)} %param.16) | copy-start | bytes 1572868
  202.4 3.1 copy-start.8
  214.3 97.6 %all-to-all-start.1 = ((bf16[32,28,2048]{2,1,0:T(8,128)(2,1)}), bf16[32,28,2048]{2,1,0:T(8,128)(2,1)}, u32[]{:S(2)}, u32[]{:S(2)}) async-start(bf16[32,28,2048]{2,1,0:T(8,128)(2,1)} %reshape.272), calls=%async_computation.1 | async-start | bytes 8388608 | tf_op jit(solution)/shard_map/all_to_all | solution.py:165
  218.1 112.7 %collective-permute-start.1 = (bf16[2,704,2048]{2,1,0:T(8,128)(2,1)}, bf16[2,704,2048]{2,1,0:T(8,128)(2,1)}, u32[]{:S(2)}, u32[]{:S(2)}) collective-permute-start(bf16[2,704,2048]{2,1,0:T(8,128)(2,1)} %bitcast.143), channel_id=1, source_target_pairs={{0,1},{1,0},{2,3},{3,2},{4,5},{5,4},{6,7},{7,6},{8,9},{9,8},{10,11... | collective-permute-start | bytes 17301512 | tf_op jit(solution)/shard_map/ppermute | solution.py:52
  218.3 120.9 %collective-permute-start.2 = (bf16[704,2048]{1,0:T(8,128)(2,1)}, bf16[704,2048]{1,0:T(8,128)(2,1)}, u32[]{:S(2)}, u32[]{:S(2)}) collective-permute-start(bf16[704,2048]{1,0:T(8,128)(2,1)} %bitcast.144), channel_id=1, source_target_pairs={{0,1},{1,0},{2,3},{3,2},{4,5},{5,4},{6,7},{7,6},{8,9},{9,8},{10,11... | collective-permute-start | bytes 8650760 | tf_op jit(solution)/shard_map/ppermute | solution.py:52
  317.8 9.4 %copy-start.11 = (bf16[1,704,2048]{2,1,0:T(8,128)(2,1)S(1)}, bf16[1,704,2048]{2,1,0:T(8,128)(2,1)}, u32[]{:S(2)}) copy-start(bf16[1,704,2048]{2,1,0:T(8,128)(2,1)} %param.25) | copy-start | bytes 8650756
  327.3 3.4 copy-start.3
  351.9 4.4 copy-start.7
  351.9 98.0 %all-to-all-start.2 = ((bf16[32,28,2048]{2,1,0:T(8,128)(2,1)}), bf16[32,28,2048]{2,1,0:T(8,128)(2,1)}, u32[]{:S(2)}, u32[]{:S(2)}) async-start(bf16[32,28,2048]{2,1,0:T(8,128)(2,1)} %reshape.274), calls=%async_computation.2 | async-start | bytes 8388608 | tf_op jit(solution)/shard_map/all_to_all | solution.py:176
  356.0 221.6 %all-reduce.5.cloned.1.call-start = ((), (), s32[]{:S(2)}) async-start(), calls=%async_computation.5 | async-start | bytes 131072 | tf_op jit(solution)/shard_map/psum | solution.py:197
  455.7 122.8 %copy-start.10 = (f32[2048]{0:T(1024)S(1)}, f32[2048]{0:T(1024)}, u32[]{:S(2)}) copy-start(f32[2048]{0:T(1024)} %param.26) | copy-start | bytes 24580
  459.6 127.4 %copy-start.5 = (bf16[128,2048]{1,0:T(8,128)(2,1)}, bf16[128,2048]{1,0:T(8,128)(2,1)S(1)}, u32[]{:S(2)}) copy-start(bf16[128,2048]{1,0:T(8,128)(2,1)S(1)} %fusion.40) | copy-start | bytes 1572868
  459.8 0.6 copy-start.6
  578.5 52.4 %copy-start.1 = (bf16[2,128,2048]{2,1,0:T(8,128)(2,1)S(1)}, bf16[2,128,2048]{2,1,0:T(8,128)(2,1)}, u32[]{:S(2)}) copy-start(bf16[2,128,2048]{2,1,0:T(8,128)(2,1)} %param.20) | copy-start | bytes 3145732
Sparse Core Ops, SparseCore 0:
  10.7 76.0 all-gather.4
  89.6 71.6 all-gather.6
  460.6 116.8 all-reduce.4
